TPU v7x, 128 devices: a whole 4x4x4 slice. The times are simulated.
128 devices in a mesh: pix: 8 (over y_hi, z), tm: 16 (over x, y_lo, core).
Axes of the slice: x: 4, y: 4 (y_hi: 2, y_lo: 2; y = y_hi * 2 + y_lo), z: 4, core: 2. Of those that a mesh axis runs over, the one named last changes fastest.
Arguments:
- frames: float32 [16, 192, 12288], P('tm', 'pix'), may hold values from 0.05 to 5
- pixel_order: int32 [12288], replicated, may hold values from 0 to 12287, each once
- cycle_sizes: int32 [64], replicated, may hold values from 1 to 384, 12288 in all
- kernel: float32 [5], replicated, may hold values from 0.1 to 1
Outputs:
- correlation: float32 [64, 3072, 3072], P('pix', 'tm')
Inputs may be any that keep to these rules, and one draw needn't show every extreme that they name: `cycle_sizes`: every cycle has one or more pixels, the sizes sum to 12288, and one cycle has exactly 384.
All inputs are finite; a program needn't handle non-finite values.
Results may differ from a plain program's by a relative error of at most 0.00005.
Values sent between devices are 32-bit elements; how exact they have to be, the bound alone decides.
No kernel may reach another device: no remote copies, remote signals or barrier semaphores. Data moves between devices by JAX's collectives and lax.ppermute only.
A program may use at most 256 MiB of HBM per device.

v0:
```python
import jax
import jax.numpy as jnp
from jax import lax
from jax.sharding import PartitionSpec as P

REACH = 2


def with_halo(block, sides, width):
    for axis, dim in sides:
        count = lax.axis_size(axis)
        forward = [(i, i + 1) for i in range(count - 1)]
        backward = [(target, source) for source, target in forward]
        low = lax.ppermute(
            lax.slice_in_dim(block, block.shape[dim] - width, None, axis=dim), axis, forward
        )
        high = lax.ppermute(lax.slice_in_dim(block, 0, width, axis=dim), axis, backward)
        block = jnp.concatenate([low, block, high], axis=dim)
    return block


def correlate(left, left_total, right, scale):
    product = jnp.einsum(
        "rct,rcs->rts",
        left,
        right,
        precision=lax.Precision.HIGHEST,
        preferred_element_type=jnp.float32,
    )
    right_total = jnp.sum(right, axis=1)
    return product * scale[:, None, None] / (left_total[:, :, None] * right_total[:, None, :])


def per_device(frames, pixel_order, cycle_sizes, kernel):
    block = frames[0]
    cycles = cycle_sizes.shape[0]
    pixels = block.shape[1]
    cap = 2 * pixels // cycles
    starts = jnp.cumsum(cycle_sizes) - cycle_sizes
    slots = jnp.arange(cap, dtype=jnp.int32)
    where_idx = jnp.minimum(starts[:, None] + slots[None, :], pixels - 1)
    valid = slots[None, :] < cycle_sizes[:, None]
    columns = pixel_order[where_idx]
    flat = jnp.transpose(block)
    picked = jnp.where(valid[:, :, None], flat[columns], 0.0)
    local = lax.all_to_all(picked, "pix", split_axis=0, concat_axis=2, tiled=True)
    owned = local.shape[0]
    tblk = local.shape[2]
    scale = lax.dynamic_slice_in_dim(cycle_sizes, lax.axis_index("pix") * owned, owned).astype(
        jnp.float32
    )
    own_total = jnp.sum(local, axis=1)
    normed = correlate(local, own_total, lax.all_gather(local, "tm", axis=2, tiled=True), scale)
    count = normed.shape[2]
    padded = jnp.pad(normed, ((0, 0), (0, 0), (REACH, REACH)))
    across = kernel[0] * padded[:, :, 0:count]
    for shift_step in range(1, 2 * REACH + 1):
        across = across + kernel[shift_step] * padded[:, :, shift_step : shift_step + count]
    rimmed = with_halo(across, (("tm", 1),), REACH)
    result = kernel[0] * rimmed[:, 0:tblk]
    for shift_step in range(1, 2 * REACH + 1):
        result = result + kernel[shift_step] * rimmed[:, shift_step : shift_step + tblk]
    return result


def solution(mesh):
    placed = (P("tm", "pix", None), P(), P(), P())
    return jax.shard_map(
        per_device, mesh=mesh, in_specs=placed, out_specs=P("pix", "tm", None), check_vma=False
    )
```

profile of v0, /device:TPU:1, one launch (start us, length us, event | category | flops | bytes accessed | tf_op | source)
XLA Modules:
  0.0 637.4 jit_solution(14035396235880347617)
XLA Ops:
  6.5 0.0 copy-start
  6.5 0.0 all-gather.2.cloned.1.call-start
  6.5 4.9 copy.15
  11.4 0.7 iota_compare_fusion
  12.2 0.7 copy.16
  12.9 0.1 reduce-window.9
  13.0 0.1 reduce.1
  13.1 0.7 sub.3
  13.8 0.1 compare_select_fusion.1
  13.9 0.0 copy-done
  13.9 135.5 %gather_fusion = s32[24576]{0:T(1024)S(1)} fusion(s32[12288]{0:T(1024)S(1)} %copy-done, s32[24576]{0:T(1024)S(1)} %broadcast_clamp_fusion), kind=kCustom, calls=%fused_computation | custom fusion | bytes 294912 | tf_op jit(solution)/shard_map/gather | solution.py:43
  149.6 84.8 %gather_fusion.1 = f32[24576,24]{1,0:T(8,128)} fusion(f32[12288,24]{1,0:T(8,128)} %bitcast.20, s32[24576]{0:T(1024)S(1)} %broadcast_clamp_fusion.1), kind=kCustom, calls=%fused_computation.1 | custom fusion | bytes 4816896 | tf_op jit(solution)/shard_map/gather | solution.py:45
  234.4 0.0 copy-start.4
  234.4 0.0 copy-start.3
  234.4 7.7 %copy.17 = f32[64,384,24]{1,2,0:T(8,128)S(1)} copy(f32[64,384,24]{2,1,0:T(8,128)} %bitcast.21) | data formatting | bytes 4718592 | tf_op jit(solution)/shard_map/gather | solution.py:45
  242.1 0.3 broadcast_select_fusion
  242.4 38.0 %all_to_all.18 = f32[64,384,24]{1,2,0:T(8,128)S(1)} all-to-all(f32[64,384,24]{1,2,0:T(8,128)S(1)} %broadcast_select_fusion), channel_id=1, replica_groups=mesh['pix'=8,'tm'=16] {'pix'}, dimensions={0} | all-to-all | bytes 4718592 | tf_op jit(solution)/shard_map/all_to_all | solution.py:46
  280.4 1.6 copy.18
  282.0 0.0 all-gather.2.cloned.1.call-update
  282.0 0.0 copy-done.4
  282.0 0.1 dynamic-slice_convert_fusion
  282.1 0.0 copy-done.3
  282.1 0.7 fusion.12
  282.7 0.3 reduce_sum.18
  283.0 0.1 mul.80
  283.1 0.0 copy-start.2
  283.1 188.8 %all-gather.2.cloned.1.call-done = f32[8,384,3072]{1,2,0:T(8,128)} async-done(((f32[8,384,192]{1,2,0:T(8,128)}), f32[8,384,3072]{1,2,0:T(8,128)}) %all-gather.2.cloned.1.call-update) | async-done | bytes 37748752 | tf_op jit(solution)/shard_map/all_gather | solution.py:53
  471.9 17.3 %reduce_sum.19 = f32[8,3072]{1,0:T(8,128)S(1)} reduce(f32[8,384,3072]{1,2,0:T(8,128)} %all-gather.2.cloned.1.call-done, f32[]{:T(128)} %constant.6.clone.1), dimensions={1}, to_apply=%region_2.3 | reduce | flops 9412608 | bytes 37847044 | tf_op jit(solution)/shard_map/reduce_sum | solution.py:30
  489.2 0.0 copy-done.2
  489.2 47.2 %multiply_divide_fusion = f32[8,192,3072]{2,1,0:T(8,128)} fusion(f32[8,3072]{1,0:T(8,128)S(1)} %reduce_sum.19, f32[8,192]{1,0:T(8,128)S(1)} %mul.80, f32[8]{0:T(128)S(1)} %dynamic-slice_convert_fusion, f32[8,384,192]{1,2,0:T(8,128)S(1)} %bitcast.25, f32[8,384,3072]{1,2,0:T(8,128)} %all-gather.2.cloned.1.call-done), kind=kOutput, calls=%fused_computation.21 | convolution fusion | flops 21757427712 | bytes 59086880 | tf_op jit(solution)/shard_map/rct,rcs->rts/dot_general | solution.py:23
  536.4 41.1 %multiply_add_fusion = f32[8,192,3072]{2,1,0:T(8,128)} fusion(f32[8,192,3072]{2,1,0:T(8,128)} %multiply_divide_fusion, f32[]{:T(128)} %bitcast.12, f32[]{:T(128)} %bitcast.11, f32[]{:T(128)} %bitcast.10, f32[]{:T(128)} %bitcast.9, f32[]{:T(128)} %bitcast), kind=kLoop, calls=%fused_computation.18 | loop fusion | flops 42467328 | bytes 37748756 | tf_op jit(solution)/shard_map/add | solution.py:58
  577.5 1.5 fusion.11
  579.0 3.2 collective-permute-start
  582.2 0.0 copy-start.1
  582.3 2.1 collective-permute-start.1
  584.3 0.5 collective-permute-done
  584.8 4.5 collective-permute-done.1
  589.4 41.1 %fusion.3 = f32[8,192,3072]{2,1,0:T(8,128)} fusion(f32[8,192,3072]{2,1,0:T(8,128)} %multiply_add_fusion, f32[8,2,3072]{2,1,0:T(2,128)S(1)} %collective-permute-done.1, f32[8,2,3072]{2,1,0:T(2,128)S(1)} %collective-permute-done, f32[]{:T(128)} %bitcast.12, f32[]{:T(128)} %bitcast.11, f32[]{:T(128)} %bitcast.10, f32[]{:T(128)} %bitcast.9, f32[]{:T(128)} %bitcast), kind=kLoop, calls=%fused_computation.9 | loop fusion | flops 61341696 | bytes 38141972 | tf_op jit(solution)/shard_map/add | solution.py:62
  630.5 0.0 copy-done.1
  (7 shorter events, 0.1 us)
Async XLA Ops:
  6.5 7.4 %copy-start = (s32[12288]{0:T(1024)S(1)}, s32[12288]{0:T(1024)}, u32[]{:S(2)}) copy-start(s32[12288]{0:T(1024)} %param.5) | copy-start | bytes 147460
  6.5 465.3 %all-gather.2.cloned.1.call-start = ((), (), s32[]{:S(2)}) async-start(), calls=%async_computation.1 | async-start | bytes 40108032 | tf_op jit(solution)/shard_map/all_gather | solution.py:53
  234.4 47.5 %copy-start.4 = (s32[64]{0:T(128)S(1)}, s32[64]{0:T(128)}, u32[]{:S(2)}) copy-start(s32[64]{0:T(128)} %param.6) | copy-start | bytes 772
  234.4 47.6 %copy-start.3 = (f32[5]{0:T(128)S(1)}, f32[5]{0:T(128)}, u32[]{:S(2)}) copy-start(f32[5]{0:T(128)} %param.7) | copy-start | bytes 64
  283.1 206.1 %copy-start.2 = (f32[8,384,8,24]{1,3,2,0:T(8,128)S(1)}, f32[8,384,8,24]{1,3,2,0:T(8,128)}, u32[]{:S(2)}) copy-start(f32[8,384,8,24]{1,3,2,0:T(8,128)} %copy.18) | copy-start | bytes 7077892
  579.0 5.8 collective-permute-start
  582.2 48.3 %copy-start.1 = (s32[12288]{0:T(1024)S(1)}, s32[12288]{0:T(1024)}, u32[]{:S(2)}) copy-start(s32[12288]{0:T(1024)} %param.5) | copy-start | bytes 147460
  582.3 7.1 %collective-permute-start.1 = (f32[8,2,3072]{2,1,0:T(2,128)S(1)}, f32[8,2,3072]{2,1,0:T(2,128)S(1)}, u32[]{:S(2)}, u32[]{:S(2)}) collective-permute-start(f32[8,2,3072]{2,1,0:T(2,128)S(1)} %get-tuple-element.6), channel_id=1, source_target_pairs={{1,0},{2,1},{3,2},{4,3},{5,4},{6,5},{7,6},{8,7},{9,8},{10,9},{11,1... | collective-permute-start | bytes 589832 | tf_op jit(solution)/shard_map/ppermute | solution.py:17
Sparse Core Ops, SparseCore 0:
  282.1 189.7 all-gather.1
where the time goes:
time: 638 us; the launch traced here: 637 us
  local copies, waits for them, and re-layouts  238 us (37%)
  waiting for transfers between devices  194 us (30%)
  other arithmetic  102 us (16%)
  matrix products  47.2 us (7%)
  blocking collectives  38 us (6%)
  between operations  13.6 us (2%)
    all_gather x1, waiting for transfers between devices, per_device(): lax.all_gather(local, 'tm', axis=2, tiled=True)  189 us
    gather x2, local copies, waits for them, and re-layouts, per_device(): columns = pixel_order[where_idx]  136 us
    gather x2, local copies, waits for them, and re-layouts, per_device(): picked = jnp.where(valid[:, :, None], flat[columns], 0.0)  92.5 us
    dot_general x1, matrix products, correlate(): jnp.einsum('rct,rcs->rts', left, right, precision=lax.Precision.HIGHEST,...  47.2 us
    add x1, other arithmetic, per_device(): result + kernel[shift_step] * rimmed[:, shift_step:shift_step + tblk]  41.1 us
    add x1, other arithmetic, per_device(): across + kernel[shift_step] * padded[:, :, shift_step:shift_step + count]  41.1 us
    all_to_all x1, blocking collectives, per_device(): lax.all_to_all(picked, 'pix', split_axis=0, concat_axis=2, tiled=True)  38 us
    reduce_sum x1, other arithmetic, correlate(): right_total = jnp.sum(right, axis=1)  17.3 us
  transfers between devices with their start and end apart: 3, of which 3 were waited for; matrix products, arithmetic and copies ran while one was open for 0% of the time, Pallas kernels for 0%

commit v1 on v0

--- a/solution.py
+++ b/solution.py
@@ -32,6 +32,15 @@
 
 
 def per_device(frames, pixel_order, cycle_sizes, kernel):
+
+    def yards_perform(buf, chip_axis, dimension_no, k_dim):
+        return jnp.concatenate(
+            jax.lax.all_to_all(
+                jnp.stack(jnp.split(buf, jax.lax.axis_size(chip_axis), axis=k_dim)), chip_axis, 0, 0
+            ),
+            axis=dimension_no,
+        )
+
     block = frames[0]
     cycles = cycle_sizes.shape[0]
     pixels = block.shape[1]
@@ -43,7 +52,7 @@
     columns = pixel_order[where_idx]
     flat = jnp.transpose(block)
     picked = jnp.where(valid[:, :, None], flat[columns], 0.0)
-    local = lax.all_to_all(picked, "pix", split_axis=0, concat_axis=2, tiled=True)
+    local = yards_perform(picked, "pix", 2, 0)
     owned = local.shape[0]
     tblk = local.shape[2]
     scale = lax.dynamic_slice_in_dim(cycle_sizes, lax.axis_index("pix") * owned, owned).astype(

time: 638 us -> 638 us (level)
  no operation moved by 1% of the time
where the time goes in v1:
time: 638 us
  local copies, waits for them, and re-layouts  238 us (37%)
  waiting for transfers between devices  194 us (30%)
  other arithmetic  102 us (16%)
  matrix products  47.2 us (7%)
  blocking collectives  38 us (6%)
  between operations  13.6 us (2%)
    all_gather x1, waiting for transfers between devices, per_device(): lax.all_gather(local, 'tm', axis=2, tiled=True)  189 us
    gather x2, local copies, waits for them, and re-layouts, per_device(): columns = pixel_order[where_idx]  136 us
    gather x2, local copies, waits for them, and re-layouts, per_device(): picked = jnp.where(valid[:, :, None], flat[columns], 0.0)  92.5 us
    dot_general x1, matrix products, correlate(): jnp.einsum('rct,rcs->rts', left, right, precision=lax.Precision.HIGHEST,...  47.2 us
    add x1, other arithmetic, per_device(): result + kernel[shift_step] * rimmed[:, shift_step:shift_step + tblk]  41.1 us
    add x1, other arithmetic, per_device(): across + kernel[shift_step] * padded[:, :, shift_step:shift_step + count]  41.1 us
    all_to_all x1, blocking collectives, yards_perform(): jax.lax.all_to_all(jnp.stack(jnp.split(buf, jax.lax.axis_size(chip_axis),...  38 us
    reduce_sum x1, other arithmetic, correlate(): right_total = jnp.sum(right, axis=1)  17.3 us
  transfers between devices with their start and end apart: 3, of which 3 were waited for; matrix products, arithmetic and copies ran while one was open for 0% of the time, Pallas kernels for 0%

profile of v1, /device:TPU:1, one launch (start us, length us, event | category | flops | bytes accessed | tf_op | source)
XLA Modules:
  0.0 637.6 jit_solution(10149181997880742596)
XLA Ops:
  6.5 0.0 copy-start
  6.5 0.0 all-gather.2.cloned.1.call-start
  6.5 4.9 copy.33
  11.4 0.7 iota_compare_fusion
  12.2 0.7 copy.34
  12.9 0.1 reduce-window.9
  13.0 0.1 reduce.1
  13.1 0.7 sub.3
  13.8 0.1 compare_select_fusion.1
  13.9 0.0 copy-done
  13.9 135.5 %gather_fusion = s32[24576]{0:T(1024)S(1)} fusion(s32[12288]{0:T(1024)S(1)} %copy-done, s32[24576]{0:T(1024)S(1)} %broadcast_clamp_fusion), kind=kCustom, calls=%fused_computation | custom fusion | bytes 294912 | tf_op jit(solution)/shard_map/gather | solution.py:52
  149.6 84.8 %gather_fusion.1 = f32[24576,24]{1,0:T(8,128)} fusion(f32[12288,24]{1,0:T(8,128)} %bitcast.51, s32[24576]{0:T(1024)S(1)} %broadcast_clamp_fusion.1), kind=kCustom, calls=%fused_computation.1 | custom fusion | bytes 4816896 | tf_op jit(solution)/shard_map/gather | solution.py:54
  234.4 0.0 copy-start.4
  234.4 0.0 copy-start.3
  234.4 7.7 %copy.35 = f32[64,384,24]{1,2,0:T(8,128)S(1)} copy(f32[64,384,24]{2,1,0:T(8,128)} %bitcast.52) | data formatting | bytes 4718592 | tf_op jit(solution)/shard_map/gather | solution.py:54
  242.1 0.3 broadcast_select_fusion
  242.6 38.0 %all_to_all.5 = f32[8,8,384,24]{2,3,1,0:T(8,128)S(1)} all-to-all(f32[8,8,384,24]{2,3,1,0:T(8,128)S(1)} %fusion.11), channel_id=1, replica_groups=mesh['pix'=8,'tm'=16] {'pix'}, dimensions={0} | all-to-all | bytes 4718592 | tf_op jit(solution)/shard_map/all_to_all | solution.py:38
  280.6 1.6 copy.36
  282.2 0.0 all-gather.2.cloned.1.call-update
  282.2 0.0 copy-done.4
  282.2 0.1 dynamic-slice_convert_fusion
  282.3 0.0 copy-done.3
  282.3 0.7 fusion.20
  283.0 0.3 bitcast_reduce_fusion
  283.3 0.1 mul.80
  283.3 0.0 copy-start.2
  283.3 188.8 %all-gather.2.cloned.1.call-done = f32[8,384,3072]{1,2,0:T(8,128)} async-done(((f32[8,384,192]{1,2,0:T(8,128)}), f32[8,384,3072]{1,2,0:T(8,128)}) %all-gather.2.cloned.1.call-update) | async-done | bytes 37748752 | tf_op jit(solution)/shard_map/all_gather | solution.py:62
  472.1 17.3 %reduce_sum.19 = f32[8,3072]{1,0:T(8,128)S(1)} reduce(f32[8,384,3072]{1,2,0:T(8,128)} %all-gather.2.cloned.1.call-done, f32[]{:T(128)} %constant.6.clone.1), dimensions={1}, to_apply=%region_2.3 | reduce | flops 9412608 | bytes 37847044 | tf_op jit(solution)/shard_map/reduce_sum | solution.py:30
  489.4 0.0 copy-done.2
  489.4 47.2 %multiply_divide_fusion = f32[8,192,3072]{2,1,0:T(8,128)} fusion(f32[8,3072]{1,0:T(8,128)S(1)} %reduce_sum.19, f32[8,192]{1,0:T(8,128)S(1)} %mul.80, f32[8]{0:T(128)S(1)} %dynamic-slice_convert_fusion, f32[8,384,192]{1,2,0:T(8,128)S(1)} %bitcast.55, f32[8,384,3072]{1,2,0:T(8,128)} %all-gather.2.cloned.1.call-done), kind=kOutput, calls=%fused_computation.21 | convolution fusion | flops 21757427712 | bytes 59086880 | tf_op jit(solution)/shard_map/rct,rcs->rts/dot_general | solution.py:23
  536.7 41.1 %multiply_add_fusion = f32[8,192,3072]{2,1,0:T(8,128)} fusion(f32[8,192,3072]{2,1,0:T(8,128)} %multiply_divide_fusion, f32[]{:T(128)} %bitcast.18, f32[]{:T(128)} %bitcast.17, f32[]{:T(128)} %bitcast.16, f32[]{:T(128)} %bitcast.15, f32[]{:T(128)} %bitcast), kind=kLoop, calls=%fused_computation.18 | loop fusion | flops 42467328 | bytes 37748756 | tf_op jit(solution)/shard_map/add | solution.py:67
  577.7 1.5 fusion.19
  579.2 3.2 collective-permute-start
  582.5 0.0 copy-start.1
  582.5 2.1 collective-permute-start.1
  584.6 0.5 collective-permute-done
  585.1 4.5 collective-permute-done.1
  589.6 41.1 %fusion.3 = f32[8,192,3072]{2,1,0:T(8,128)} fusion(f32[8,192,3072]{2,1,0:T(8,128)} %multiply_add_fusion, f32[8,2,3072]{2,1,0:T(2,128)S(1)} %collective-permute-done.1, f32[8,2,3072]{2,1,0:T(2,128)S(1)} %collective-permute-done, f32[]{:T(128)} %bitcast.18, f32[]{:T(128)} %bitcast.17, f32[]{:T(128)} %bitcast.16, f32[]{:T(128)} %bitcast.15, f32[]{:T(128)} %bitcast), kind=kLoop, calls=%fused_computation.9 | loop fusion | flops 61341696 | bytes 38141972 | tf_op jit(solution)/shard_map/add | solution.py:71
  630.8 0.0 copy-done.1
  (15 shorter events, 0.3 us)
Async XLA Ops:
  6.5 7.4 %copy-start = (s32[12288]{0:T(1024)S(1)}, s32[12288]{0:T(1024)}, u32[]{:S(2)}) copy-start(s32[12288]{0:T(1024)} %param.5) | copy-start | bytes 147460
  6.5 465.6 %all-gather.2.cloned.1.call-start = ((), (), s32[]{:S(2)}) async-start(), calls=%async_computation.1 | async-start | bytes 40108032 | tf_op jit(solution)/shard_map/all_gather | solution.py:62
  234.4 47.8 %copy-start.4 = (s32[64]{0:T(128)S(1)}, s32[64]{0:T(128)}, u32[]{:S(2)}) copy-start(s32[64]{0:T(128)} %param.6) | copy-start | bytes 772
  234.4 47.9 %copy-start.3 = (f32[5]{0:T(128)S(1)}, f32[5]{0:T(128)}, u32[]{:S(2)}) copy-start(f32[5]{0:T(128)} %param.7) | copy-start | bytes 64
  283.3 206.1 %copy-start.2 = (f32[8,384,8,24]{1,3,2,0:T(8,128)S(1)}, f32[8,384,8,24]{1,3,2,0:T(8,128)}, u32[]{:S(2)}) copy-start(f32[8,384,8,24]{1,3,2,0:T(8,128)} %copy.36) | copy-start | bytes 7077892
  579.2 5.8 collective-permute-start
  582.5 48.3 %copy-start.1 = (s32[12288]{0:T(1024)S(1)}, s32[12288]{0:T(1024)}, u32[]{:S(2)}) copy-start(s32[12288]{0:T(1024)} %param.5) | copy-start | bytes 147460
  582.5 7.1 %collective-permute-start.1 = (f32[8,2,3072]{2,1,0:T(2,128)S(1)}, f32[8,2,3072]{2,1,0:T(2,128)S(1)}, u32[]{:S(2)}, u32[]{:S(2)}) collective-permute-start(f32[8,2,3072]{2,1,0:T(2,128)S(1)} %get-tuple-element.6), channel_id=1, source_target_pairs={{1,0},{2,1},{3,2},{4,3},{5,4},{6,5},{7,6},{8,7},{9,8},{10,9},{11,1... | collective-permute-start | bytes 589832 | tf_op jit(solution)/shard_map/ppermute | solution.py:17
Sparse Core Ops, SparseCore 0:
  282.3 189.7 all-gather.1
